TPU v7x, 32 devices: a whole 2x2x4 slice. The times are simulated.
32 devices in a mesh: groups: 2 (over x), seq: 8 (over z, y), chan: 2 (over core).
Axes of the slice: x: 2, y: 2, z: 4, core: 2. Of those that a mesh axis runs over, the one named last changes fastest.
Arguments:
- cached_input: bfloat16 [2048, 4096], P(('groups', 'seq'), 'chan'), parts along dimension 0, may hold values from -6 to 6
- cached_gate: bfloat16 [2048, 4096], P(('groups', 'seq'), 'chan'), parts along dimension 0, may hold values from -6 to 6
- out_grad: bfloat16 [2048, 4096], P(('groups', 'seq'), 'chan'), parts along dimension 0, may hold values from -1.75 to 1.75
- filter_taps: bfloat16 [1024, 32], P('seq', 'chan'), may hold values from -6 to 6
- skip_gain: float32 [4096], P('chan'), may hold values from -1 to 1
Outputs:
- input_grad: bfloat16 [2048, 4096], P(('groups', 'seq'), 'chan'), parts along dimension 0
- filter_grad: float32 [2048, 32], P(('groups', 'seq'), 'chan'), parts along dimension 0
There are 2 independent parts, one for each index of `groups`. A program takes and returns all parts, laid end to end along the dimension named above; an argument that names none is the same for every part. Nothing has to cross between parts.
All inputs are finite; a program needn't handle non-finite values.
Results may differ from a plain program's by a relative error of at most 0.005.
Values may be sent and summed in bfloat16 or wider, within the bound.
No kernel may reach another device: no remote copies, remote signals or barrier semaphores. Data moves between devices by JAX's collectives and lax.ppermute only.
A program may use at most 64 MiB of HBM per device.

v0:
```python
import math
import jax
import jax.numpy as jnp
from jax import lax
from jax.sharding import PartitionSpec as P

lag_group = 4


def toeplitz_blocks(windows, block_rows):
    flipped = windows[..., ::-1]
    tiled = jnp.tile(flipped, (1, 1, block_rows))
    trimmed = tiled[..., : block_rows * (2 * block_rows - 1)]
    shaped = trimmed.reshape(windows.shape[0], windows.shape[1], block_rows, 2 * block_rows - 1)
    return shaped[..., block_rows - 1 : 2 * block_rows - 1]


def diagonal_sums(products, block_rows):
    flipped = products[..., ::-1]
    padded = jnp.pad(flipped, ((0, 0), (0, 0), (0, 0), (0, block_rows)))
    flattened = padded.reshape(products.shape[0], products.shape[1], 2 * block_rows * block_rows)
    trimmed = flattened[..., : block_rows * (2 * block_rows - 1)]
    shaped = trimmed.reshape(products.shape[0], products.shape[1], block_rows, 2 * block_rows - 1)
    diag_sums = jnp.sum(shaped, axis=2)
    return jnp.pad(diag_sums, ((0, 0), (0, 0), (1, 0)))


def fold_windows(window_grads, block_rows):
    front_half = jnp.pad(window_grads[..., :block_rows], ((0, 1), (0, 0), (0, 0)))
    back_half = jnp.pad(window_grads[..., block_rows:], ((1, 0), (0, 0), (0, 0)))
    joined = front_half + back_half
    return jnp.transpose(joined, (1, 0, 2)).reshape(window_grads.shape[1], -1)


def lag_table(taps_all, block_rows):
    return jnp.pad(jnp.transpose(taps_all), ((0, 0), (block_rows, lag_group * block_rows)))


def lag_sweep(
    blocks, base_block, block_count, sources, tap_table, block_rows, trip_count, seq_count
):
    filters = sources.shape[2]
    group_width = sources.shape[3]

    def advance(lag_step, state_pair):
        input_acc, lag_acc = state_pair
        lag_start = lag_step * lag_group
        stacked = jnp.stack(
            [
                lax.dynamic_slice_in_dim(blocks, base_block + lag_start + offset, block_count, 0)
                for offset in range(lag_group)
            ],
            axis=1,
        )
        lag_span = lax.dynamic_slice_in_dim(
            tap_table, lag_start * block_rows, (lag_group + 1) * block_rows, 1
        )
        windows = jnp.stack(
            [
                lag_span[:, offset * block_rows : (offset + 2) * block_rows]
                for offset in range(lag_group)
            ],
            axis=0,
        )
        toeplitz = toeplitz_blocks(windows, block_rows)
        input_acc = input_acc + jnp.einsum(
            "kfts,iktfg->isfg", toeplitz, stacked, preferred_element_type=jnp.float32
        )
        products = jnp.einsum(
            "iktfg,isfg->kfts", stacked, sources, preferred_element_type=jnp.float32
        )
        folded = fold_windows(diagonal_sums(products, block_rows), block_rows)
        previous = lax.dynamic_slice_in_dim(
            lag_acc, lag_start * block_rows, (lag_group + 1) * block_rows, 1
        )
        lag_acc = lax.dynamic_update_slice_in_dim(
            lag_acc, previous + folded, lag_start * block_rows, 1
        )
        return (input_acc, lag_acc)

    initial = (
        jnp.zeros((block_count, block_rows, filters, group_width), jnp.float32),
        jnp.zeros((filters, (seq_count + 1 + lag_group) * block_rows), jnp.float32),
    )
    return lax.fori_loop(0, trip_count, advance, initial)


def per_device(cached_input, cached_gate, out_grad, filter_taps, skip_gain):
    block_rows = cached_input.shape[0]
    chan_width = cached_input.shape[1]
    filters = filter_taps.shape[1]
    group_width = chan_width // filters
    seq_count = lax.axis_size("seq")
    seq_index = lax.axis_index("seq")
    length = block_rows * seq_count
    taps_scale = 1.0 / math.sqrt(length)
    gated_grad = (out_grad.astype(jnp.float32) * cached_gate.astype(jnp.float32)).astype(
        jnp.bfloat16
    )
    stretch_width = chan_width // seq_count
    moved_grad, moved_input = (
        lax.all_to_all(gated_grad, "seq", split_axis=1, concat_axis=0, tiled=True),
        lax.all_to_all(cached_input, "seq", split_axis=1, concat_axis=0, tiled=True),
    )
    taps_all = lax.all_gather(filter_taps, "seq", axis=0, tiled=True)
    stretch_filters = max(1, stretch_width // group_width)
    stretch_group = stretch_width // stretch_filters
    first_filter = seq_index * stretch_width // group_width
    stretch_taps = lax.dynamic_slice_in_dim(taps_all, first_filter, stretch_filters, 1)
    shaped_grad = moved_grad.reshape(seq_count, block_rows, stretch_filters, stretch_group)
    blocks = jnp.pad(shaped_grad, ((0, seq_count - 1 + lag_group), (0, 0), (0, 0), (0, 0)))
    sources = moved_input.reshape(seq_count, block_rows, stretch_filters, stretch_group)
    trip_count = (seq_count + lag_group - 1) // lag_group
    input_acc, lag_acc = lag_sweep(
        blocks,
        0,
        seq_count,
        sources,
        lag_table(stretch_taps, block_rows),
        block_rows,
        trip_count,
        seq_count,
    )
    stretch_gain = lax.dynamic_slice_in_dim(skip_gain, seq_index * stretch_width, stretch_width, 0)
    conv_grad = input_acc.reshape(length, stretch_width) * taps_scale
    local_grad = (conv_grad + stretch_gain[None, :] * moved_grad.astype(jnp.float32)).astype(
        jnp.bfloat16
    )
    input_grad = lax.all_to_all(local_grad, "seq", split_axis=0, concat_axis=1, tiled=True)
    stretch_term = jnp.transpose(lag_acc[:, block_rows : block_rows + length]) * taps_scale
    lag_term = lax.dynamic_update_slice_in_dim(
        jnp.zeros((length, filters), jnp.float32), stretch_term, first_filter, 1
    )
    filter_grad = lax.psum_scatter(lag_term, "seq", scatter_dimension=0, tiled=True)
    return (input_grad, filter_grad)


def solution(mesh):
    return jax.shard_map(
        per_device,
        mesh=mesh,
        in_specs=(
            P(("groups", "seq"), "chan"),
            P(("groups", "seq"), "chan"),
            P(("groups", "seq"), "chan"),
            P("seq", "chan"),
            P("chan"),
        ),
        out_specs=(P(("groups", "seq"), "chan"), P(("groups", "seq"), "chan")),
        check_vma=False,
    )
```

profile of v0, /device:TPU:0, one launch (start us, length us, event | category | flops | bytes accessed | tf_op | source)
XLA Modules:
  0.0 169.5 jit_solution(654285990207121783)
XLA Ops:
  7.2 1.3 multiply_convert_fusion
  9.5 7.3 %all-to-all-start = ((bf16[128,8,256]{0,2,1:T(8,128)(2,1)}), bf16[128,8,256]{0,2,1:T(8,128)(2,1)S(1)}, u32[]{:S(2)}, u32[]{:S(2)}) async-start(bf16[128,8,256]{0,2,1:T(8,128)(2,1)} %bitcast), calls=%async_computation | async-start | bytes 1048576 | tf_op jit(solution)/shard_map/all_to_all | solution.py:102
  16.8 1.0 copy.22
  17.8 13.4 %all-to-all-done = bf16[128,8,256]{0,2,1:T(8,128)(2,1)S(1)} async-done(((bf16[128,8,256]{0,2,1:T(8,128)(2,1)}), bf16[128,8,256]{0,2,1:T(8,128)(2,1)S(1)}, u32[]{:S(2)}, u32[]{:S(2)}) %all-to-all-start) | async-done | bytes 524320 | tf_op jit(solution)/shard_map/all_to_all | solution.py:102
  31.3 3.6 %all-to-all-start.1 = ((bf16[128,8,256]{0,2,1:T(8,128)(2,1)}), bf16[128,8,256]{0,2,1:T(8,128)(2,1)S(1)}, u32[]{:S(2)}, u32[]{:S(2)}) async-start(bf16[128,8,256]{0,2,1:T(8,128)(2,1)} %bitcast.4), calls=%async_computation.1 | async-start | bytes 1048576 | tf_op jit(solution)/shard_map/all_to_all | solution.py:103
  34.9 33.2 %all_gather.3 = bf16[1024,16]{0,1:T(8,128)(2,1)S(1)} all-gather(bf16[128,16]{0,1:T(8,128)(2,1)S(1)} %copy-done.7), channel_id=1, replica_groups=mesh['groups'=2,'seq'=8,'chan'=2] {'seq'}, dimensions={0}, use_global_device_ids=true | all-gather | bytes 36864 | tf_op jit(solution)/shard_map/all_gather | solution.py:105
  69.2 1.0 copy.24
  70.2 26.8 %while.18 = (s32[]{:T(128)}, f32[8,128,2,128]{1,3,0,2:T(8,128)}, f32[2,1664]{1,0:T(2,128)S(1)}, bf16[19,128,2,128]{1,3,0,2:T(8,128)(2,1)S(1)}, bf16[2,1664]{1,0:...) while((s32[]{:T(128)}, f32[8,128,2,128]{1,3,0,2:T(8,128)}, ...), condition=%wide.region_2.3_spmd.clone, body=%wide.region_0.2_spmd.clone.sunk | while | flops 543954432 | bytes 31783416 | solution.py:85
  70.2 1.2 dynamic-slice_bitcast_fusion.6
  72.2 1.6 reshape.89
  73.8 3.1 %fusion.19 = f32[8,128,2,128]{1,3,0,2:T(8,128)} fusion(f32[8,128,2,128]{1,3,0,2:T(8,128)} %get-tuple-element.301, pred[]{:T(512)S(6)} %compare.11, bf16[8,1,128,2,128]{2,4,1,0,3:T(8,128)(2,1)S(1)} %get-tuple-element.269, bf16[8,1,128,2,128]{2,4,1,0,3:T(8,128)(2,1)} %get-tuple-element.270, bf16[8,1,128,2,128]{2,4,1,0,3:T(8,128)(2,1)} %get-tuple-element.271, ...), kind=kOutput, calls=%fused_computation.2.clone.1 | convolution fusion | flops 272105472 | bytes 4456449 | tf_op jit(solution)/shard_map/while/body/eval_jaxpr/kfts,iktfg->isfg/dot_general | solution.py:66
  76.9 1.1 convolution_bitcast_fusion.3
  79.4 1.1 slice.123
  80.4 2.8 %reshape.91 = f32[4,2,128,255]{3,2,0,1:T(8,128)S(1)} reshape(f32[4,2,32640]{2,0,1:T(4,128)} %slice.123) | data formatting | bytes 2088960 | tf_op jit(solution)/shard_map/while/body/eval_jaxpr/reshape | solution.py:23
  83.5 1.2 dynamic-slice_bitcast_fusion.6
  85.5 1.6 reshape.89
  87.1 3.4 %fusion.19 = f32[8,128,2,128]{1,3,0,2:T(8,128)} fusion(f32[8,128,2,128]{1,3,0,2:T(8,128)} %get-tuple-element.301, pred[]{:T(512)S(6)} %compare.11, bf16[8,1,128,2,128]{2,4,1,0,3:T(8,128)(2,1)S(1)} %get-tuple-element.269, bf16[8,1,128,2,128]{2,4,1,0,3:T(8,128)(2,1)} %get-tuple-element.270, bf16[8,1,128,2,128]{2,4,1,0,3:T(8,128)(2,1)} %get-tuple-element.271, ...), kind=kOutput, calls=%fused_computation.2.clone.1 | convolution fusion | flops 272105472 | bytes 4456449 | tf_op jit(solution)/shard_map/while/body/eval_jaxpr/kfts,iktfg->isfg/dot_general | solution.py:66
  90.5 1.1 convolution_bitcast_fusion.3
  93.0 1.1 slice.123
  94.0 2.8 %reshape.91 = f32[4,2,128,255]{3,2,0,1:T(8,128)S(1)} reshape(f32[4,2,32640]{2,0,1:T(4,128)} %slice.123) | data formatting | bytes 2088960 | tf_op jit(solution)/shard_map/while/body/eval_jaxpr/reshape | solution.py:23
  97.1 1.4 copy_multiply_fusion
  99.5 3.5 %all-to-all-start.2 = ((bf16[8,128,256]{1,2,0:T(8,128)(2,1)}), bf16[8,128,256]{1,2,0:T(8,128)(2,1)S(1)}, u32[]{:S(2)}, u32[]{:S(2)}) async-start(bf16[8,128,256]{1,2,0:T(8,128)(2,1)} %fusion.9), calls=%async_computation.2 | async-start | bytes 1048576 | tf_op jit(solution)/shard_map/all_to_all | solution.py:129
  104.0 9.2 %all-to-all-done.2 = bf16[8,128,256]{1,2,0:T(8,128)(2,1)S(1)} async-done(((bf16[8,128,256]{1,2,0:T(8,128)(2,1)}), bf16[8,128,256]{1,2,0:T(8,128)(2,1)S(1)}, u32[]{:S(2)}, u32[]{:S(2)}) %all-to-all-start.2) | async-done | bytes 524320 | tf_op jit(solution)/shard_map/all_to_all | solution.py:129
  114.2 48.4 %reduce-scatter.2.cloned.1.call-done = f32[128,16]{0,1:T(8,128)} async-done(((f32[1024,16]{0,1:T(8,128)}), f32[128,16]{0,1:T(8,128)}) %reduce-scatter.2.cloned.1.call-update) | async-done | bytes 8208 | tf_op jit(solution)/shard_map/reduce_scatter | solution.py:134
  (64 shorter events, 9.6 us)
Async XLA Ops:
  8.5 8.3 %copy-start.4 = (bf16[128,2048]{1,0:T(8,128)(2,1)S(1)}, bf16[128,2048]{1,0:T(8,128)(2,1)}, u32[]{:S(2)}) copy-start(bf16[128,2048]{1,0:T(8,128)(2,1)} %param.7) | copy-start | bytes 1572868
  9.5 21.8 %all-to-all-start = ((bf16[128,8,256]{0,2,1:T(8,128)(2,1)}), bf16[128,8,256]{0,2,1:T(8,128)(2,1)S(1)}, u32[]{:S(2)}, u32[]{:S(2)}) async-start(bf16[128,8,256]{0,2,1:T(8,128)(2,1)} %bitcast), calls=%async_computation | async-start | bytes 1048576 | tf_op jit(solution)/shard_map/all_to_all | solution.py:102
  16.8 18.1 %copy-start.7 = (bf16[128,16]{0,1:T(8,128)(2,1)S(1)}, bf16[128,16]{0,1:T(8,128)(2,1)}, u32[]{:S(2)}) copy-start(bf16[128,16]{0,1:T(8,128)(2,1)} %param.10) | copy-start | bytes 12292
  31.3 37.6 %copy-start.2 = (bf16[128,8,256]{0,2,1:T(8,128)(2,1)}, bf16[128,8,256]{0,2,1:T(8,128)(2,1)S(1)}, u32[]{:S(2)}) copy-start(bf16[128,8,256]{0,2,1:T(8,128)(2,1)S(1)} %all-to-all-done) | copy-start | bytes 1572868
  31.3 37.9 %all-to-all-start.1 = ((bf16[128,8,256]{0,2,1:T(8,128)(2,1)}), bf16[128,8,256]{0,2,1:T(8,128)(2,1)S(1)}, u32[]{:S(2)}, u32[]{:S(2)}) async-start(bf16[128,8,256]{0,2,1:T(8,128)(2,1)} %bitcast.4), calls=%async_computation.1 | async-start | bytes 1048576 | tf_op jit(solution)/shard_map/all_to_all | solution.py:103
  73.7 3.1 %copy-start = (bf16[8,1,128,2,128]{2,4,1,0,3:T(8,128)(2,1)S(1)}, bf16[8,1,128,2,128]{2,4,1,0,3:T(8,128)(2,1)}, u32[]{:S(2)}) copy-start(bf16[8,1,128,2,128]{2,4,1,0,3:T(8,128)(2,1)} %get-tuple-element.270) | copy-start | bytes 1572868 | tf_op jit(solution)/shard_map/while
  73.8 3.1 %copy-start.1 = (bf16[8,1,128,2,128]{2,4,1,0,3:T(8,128)(2,1)S(1)}, bf16[8,1,128,2,128]{2,4,1,0,3:T(8,128)(2,1)}, u32[]{:S(2)}) copy-start(bf16[8,1,128,2,128]{2,4,1,0,3:T(8,128)(2,1)} %get-tuple-element.271) | copy-start | bytes 1572868 | tf_op jit(solution)/shard_map/while
  73.8 3.1 %copy-start.5 = (bf16[8,128,2,128]{3,1,0,2:T(8,128)(2,1)S(1)}, bf16[8,128,2,128]{3,1,0,2:T(8,128)(2,1)}, u32[]{:S(2)}) copy-start(bf16[8,128,2,128]{3,1,0,2:T(8,128)(2,1)} %get-tuple-element.326) | copy-start | bytes 1572868 | tf_op jit(solution)/shard_map/while
  87.0 3.5 %copy-start = (bf16[8,1,128,2,128]{2,4,1,0,3:T(8,128)(2,1)S(1)}, bf16[8,1,128,2,128]{2,4,1,0,3:T(8,128)(2,1)}, u32[]{:S(2)}) copy-start(bf16[8,1,128,2,128]{2,4,1,0,3:T(8,128)(2,1)} %get-tuple-element.270) | copy-start | bytes 1572868 | tf_op jit(solution)/shard_map/while
  87.0 3.5 %copy-start.1 = (bf16[8,1,128,2,128]{2,4,1,0,3:T(8,128)(2,1)S(1)}, bf16[8,1,128,2,128]{2,4,1,0,3:T(8,128)(2,1)}, u32[]{:S(2)}) copy-start(bf16[8,1,128,2,128]{2,4,1,0,3:T(8,128)(2,1)} %get-tuple-element.271) | copy-start | bytes 1572868 | tf_op jit(solution)/shard_map/while
  87.0 3.5 %copy-start.5 = (bf16[8,128,2,128]{3,1,0,2:T(8,128)(2,1)S(1)}, bf16[8,128,2,128]{3,1,0,2:T(8,128)(2,1)}, u32[]{:S(2)}) copy-start(bf16[8,128,2,128]{3,1,0,2:T(8,128)(2,1)} %get-tuple-element.326) | copy-start | bytes 1572868 | tf_op jit(solution)/shard_map/while
  97.1 1.4 copy-start.3
  99.5 13.8 %all-to-all-start.2 = ((bf16[8,128,256]{1,2,0:T(8,128)(2,1)}), bf16[8,128,256]{1,2,0:T(8,128)(2,1)S(1)}, u32[]{:S(2)}, u32[]{:S(2)}) async-start(bf16[8,128,256]{1,2,0:T(8,128)(2,1)} %fusion.9), calls=%async_computation.2 | async-start | bytes 1048576 | tf_op jit(solution)/shard_map/all_to_all | solution.py:129
  103.0 59.7 %reduce-scatter.2.cloned.1.call-start = ((), (), s32[]{:S(2)}) async-start(), calls=%async_computation.4 | async-start | bytes 73728 | tf_op jit(solution)/shard_map/reduce_scatter | solution.py:134
  103.3 0.6 copy-start.6
Sparse Core Ops, SparseCore 0:
  107.5 55.0 reduce-scatter.1
where the time goes:
time: 170 us; the launch traced here: 169 us
  waiting for transfers between devices  71.1 us (42%)
  blocking collectives  33.2 us (20%)
  local copies, waits for them, and re-layouts  23.6 us (14%)
  starting transfers between devices  14.5 us (9%)
  between operations  14.2 us (8%)
  matrix products  8.75 us (5%)
  other arithmetic  3.94 us (2%)
    reduce_scatter x1, waiting for transfers between devices, per_device(): lax.psum_scatter(lag_term, 'seq', scatter_dimension=0, tiled=True)  48.4 us
    all_gather x1, blocking collectives, per_device(): taps_all = lax.all_gather(filter_taps, 'seq', axis=0, tiled=True)  33.2 us
    all_to_all x1, waiting for transfers between devices, per_device(): lax.all_to_all(gated_grad, 'seq', split_axis=1, concat_axis=0, tiled=True)  13.4 us
    all_to_all x1, waiting for transfers between devices, per_device(): lax.all_to_all(local_grad, 'seq', split_axis=0, concat_axis=1, tiled=True)  9.23 us
    all_to_all x1, starting transfers between devices, per_device(): lax.all_to_all(gated_grad, 'seq', split_axis=1, concat_axis=0, tiled=True)  7.28 us
    dot_general x2, matrix products, advance(): jnp.einsum('kfts,iktfg->isfg', toeplitz, stacked, preferred_element_type=...  6.53 us
    reshape x2, local copies, waits for them, and re-layouts, diagonal_sums(): trimmed.reshape(products.shape[0], products.shape[1], block_rows, 2 * blo...  5.62 us
    unnamed x14, local copies, waits for them, and re-layouts  3.72 us
  transfers between devices with their start and end apart: 4, of which 3 were waited for; matrix products, arithmetic and copies ran while one was open for 2% of the time, Pallas kernels for 0%

commit v1 on v0

--- a/solution.py
+++ b/solution.py
@@ -102,7 +102,15 @@
         lax.all_to_all(gated_grad, "seq", split_axis=1, concat_axis=0, tiled=True),
         lax.all_to_all(cached_input, "seq", split_axis=1, concat_axis=0, tiled=True),
     )
-    taps_all = lax.all_gather(filter_taps, "seq", axis=0, tiled=True)
+    ways, here = (lax.axis_size("seq"), lax.axis_index("seq"))
+    grown, reach = (filter_taps, 1)
+    while reach < ways:
+        theirs = lax.ppermute(grown, "seq", [(d, d ^ reach) for d in range(ways)])
+        mine_first = jnp.concatenate([grown, theirs], axis=0)
+        theirs_first = jnp.concatenate([theirs, grown], axis=0)
+        grown = jnp.where(here & reach == 0, mine_first, theirs_first)
+        reach = 2 * reach
+    taps_all = grown
     stretch_filters = max(1, stretch_width // group_width)
     stretch_group = stretch_width // stretch_filters
     first_filter = seq_index * stretch_width // group_width

time: 170 us -> 153 us (0.900)
  blocking collectives: 33.2 us -> 0 us
  starting transfers between devices: 14.5 us -> 22.9 us
  waiting for transfers between devices: 71.1 us -> 78.8 us
    all_gather x1 -> x0, blocking collectives: 33.2 us -> none  [per_device(): taps_all = lax.all_gather(filter_taps, 'seq', axis=0, tiled=True)]
    ppermute x0 -> x3, waiting for transfers between devices: none -> 7.67 us  [per_device(): theirs = lax.ppermute(grown, 'seq', [(d, d ^ reach) for d in range(ways)])]
    ppermute x0 -> x3, starting transfers between devices: none -> 6.82 us  [per_device(): theirs = lax.ppermute(grown, 'seq', [(d, d ^ reach) for d in range(ways)])]
    all_to_all x1, waiting for transfers between devices: 9.23 us -> 11.8 us  [per_device(): lax.all_to_all(local_grad, 'seq', split_axis=0, concat_axis=1, tiled=True)]
    reduce_scatter x1, waiting for transfers between devices: 48.4 us -> 45.9 us  [per_device(): lax.psum_scatter(lag_term, 'seq', scatter_dimension=0, tiled=True)]
  transfers between devices with their start and end apart: 4 -> 7, of which waited for: 3 -> 6; matrix products, arithmetic and copies ran while one was open for 2% -> 2% of each run, Pallas kernels for 0% -> 0%
where the time goes in v1:
time: 153 us; the launch traced here: 152 us
  waiting for transfers between devices  78.8 us (52%)
  local copies, waits for them, and re-layouts  23.6 us (15%)
  starting transfers between devices  22.9 us (15%)
  between operations  14.2 us (9%)
  matrix products  8.76 us (6%)
  other arithmetic  3.99 us (3%)
    reduce_scatter x1, waiting for transfers between devices, per_device(): lax.psum_scatter(lag_term, 'seq', scatter_dimension=0, tiled=True)  45.9 us
    all_to_all x1, waiting for transfers between devices, per_device(): lax.all_to_all(gated_grad, 'seq', split_axis=1, concat_axis=0, tiled=True)  13.4 us
    all_to_all x1, waiting for transfers between devices, per_device(): lax.all_to_all(local_grad, 'seq', split_axis=0, concat_axis=1, tiled=True)  11.8 us
    ppermute x3, waiting for transfers between devices, per_device(): theirs = lax.ppermute(grown, 'seq', [(d, d ^ reach) for d in range(ways)])  7.67 us
    all_to_all x1, starting transfers between devices, per_device(): lax.all_to_all(gated_grad, 'seq', split_axis=1, concat_axis=0, tiled=True)  7.28 us
    ppermute x3, starting transfers between devices, per_device(): theirs = lax.ppermute(grown, 'seq', [(d, d ^ reach) for d in range(ways)])  6.82 us
    dot_general x2, matrix products, advance(): jnp.einsum('kfts,iktfg->isfg', toeplitz, stacked, preferred_element_type=...  6.54 us
    reshape x2, local copies, waits for them, and re-layouts, diagonal_sums(): trimmed.reshape(products.shape[0], products.shape[1], block_rows, 2 * blo...  5.62 us
  transfers between devices with their start and end apart: 7, of which 6 were waited for; matrix products, arithmetic and copies ran while one was open for 2% of the time, Pallas kernels for 0%

profile of v1, /device:TPU:0, one launch (start us, length us, event | category | flops | bytes accessed | tf_op | source)
XLA Modules:
  0.0 152.5 jit_solution(509034260542738656)
XLA Ops:
  7.2 1.3 multiply_convert_fusion
  9.5 7.3 %all-to-all-start = ((bf16[128,8,256]{0,2,1:T(8,128)(2,1)}), bf16[128,8,256]{0,2,1:T(8,128)(2,1)S(1)}, u32[]{:S(2)}, u32[]{:S(2)}) async-start(bf16[128,8,256]{0,2,1:T(8,128)(2,1)} %bitcast), calls=%async_computation | async-start | bytes 1048576 | tf_op jit(solution)/shard_map/all_to_all | solution.py:102
  17.8 13.4 %all-to-all-done = bf16[128,8,256]{0,2,1:T(8,128)(2,1)S(1)} async-done(((bf16[128,8,256]{0,2,1:T(8,128)(2,1)}), bf16[128,8,256]{0,2,1:T(8,128)(2,1)S(1)}, u32[]{:S(2)}, u32[]{:S(2)}) %all-to-all-start) | async-done | bytes 524320 | tf_op jit(solution)/shard_map/all_to_all | solution.py:102
  31.3 3.6 %all-to-all-start.1 = ((bf16[128,8,256]{0,2,1:T(8,128)(2,1)}), bf16[128,8,256]{0,2,1:T(8,128)(2,1)S(1)}, u32[]{:S(2)}, u32[]{:S(2)}) async-start(bf16[128,8,256]{0,2,1:T(8,128)(2,1)} %bitcast.4), calls=%async_computation.1 | async-start | bytes 1048576 | tf_op jit(solution)/shard_map/all_to_all | solution.py:103
  34.9 2.0 %collective-permute-start = (bf16[128,16]{0,1:T(8,128)(2,1)S(1)}, bf16[128,16]{0,1:T(8,128)(2,1)S(1)}, u32[]{:S(2)}, u32[]{:S(2)}) collective-permute-start(bf16[128,16]{0,1:T(8,128)(2,1)S(1)} %copy-done.7), channel_id=1, source_target_pairs={{0,2},{2,0},{4,6},{6,4},{8,10},{10,8},{12,14},{14,12},{1,3},{3,1},... | collective-permute-start | bytes 12296 | tf_op jit(solution)/shard_map/ppermute | solution.py:108
  36.9 3.8 %collective-permute-done = bf16[128,16]{0,1:T(8,128)(2,1)S(1)} collective-permute-done((bf16[128,16]{0,1:T(8,128)(2,1)S(1)}, bf16[128,16]{0,1:T(8,128)(2,1)S(1)}, u32[]{:S(2)}, u32[]{:S(2)}) %collective-permute-start) | collective-permute-done | bytes 4128 | tf_op jit(solution)/shard_map/ppermute | solution.py:108
  41.6 2.9 %collective-permute-done.1 = bf16[256,16]{0,1:T(8,128)(2,1)S(1)} collective-permute-done((bf16[256,16]{0,1:T(8,128)(2,1)S(1)}, bf16[256,16]{0,1:T(8,128)(2,1)S(1)}, u32[]{:S(2)}, u32[]{:S(2)}) %collective-permute-start.1) | collective-permute-done | bytes 8224 | tf_op jit(solution)/shard_map/ppermute | solution.py:108
  44.5 4.0 %collective-permute-start.2 = (bf16[512,16]{0,1:T(8,128)(2,1)S(1)}, bf16[512,16]{0,1:T(8,128)(2,1)S(1)}, u32[]{:S(2)}, u32[]{:S(2)}) collective-permute-start(bf16[512,16]{0,1:T(8,128)(2,1)S(1)} %maximum_select_fusion), channel_id=1, source_target_pairs={{0,8},{2,10},{4,12},{6,14},{8,0},{10,2},{12,4},{14,6},{1,9},{3,11}... | collective-permute-start | bytes 49160 | tf_op jit(solution)/shard_map/ppermute | solution.py:108
  51.5 26.9 %while.18 = (s32[]{:T(128)}, f32[8,128,2,128]{1,3,0,2:T(8,128)}, f32[2,1664]{1,0:T(2,128)S(1)}, bf16[19,128,2,128]{1,3,0,2:T(8,128)(2,1)S(1)}, bf16[2,1664]{1,0:...) while((s32[]{:T(128)}, f32[8,128,2,128]{1,3,0,2:T(8,128)}, ...), condition=%wide.region_2.3_spmd.clone, body=%wide.region_0.2_spmd.clone.sunk | while | flops 543954432 | bytes 31783416 | solution.py:85
  51.5 1.2 dynamic-slice_bitcast_fusion.5
  53.5 1.6 %reshape.89 = bf16[4,2,128,255]{3,2,1,0:T(8,128)(2,1)S(1)} reshape(bf16[4,2,32640]{2,1,0:T(2,128)(2,1)S(1)} %slice.122) | data formatting | bytes 1044480 | tf_op jit(solution)/shard_map/while/body/eval_jaxpr/reshape | solution.py:14
  55.1 3.1 %fusion.22 = f32[8,128,2,128]{1,3,0,2:T(8,128)} fusion(f32[8,128,2,128]{1,3,0,2:T(8,128)} %get-tuple-element.301, pred[]{:T(512)S(6)} %compare.11, bf16[8,1,128,2,128]{2,4,1,0,3:T(8,128)(2,1)S(1)} %get-tuple-element.269, bf16[8,1,128,2,128]{2,4,1,0,3:T(8,128)(2,1)} %get-tuple-element.270, bf16[8,1,128,2,128]{2,4,1,0,3:T(8,128)(2,1)} %get-tuple-element.271, ...), kind=kOutput, calls=%fused_computation.2.clone.1 | convolution fusion | flops 272105472 | bytes 4456449 | tf_op jit(solution)/shard_map/while/body/eval_jaxpr/kfts,iktfg->isfg/dot_general | solution.py:66
  58.2 1.1 convolution_bitcast_fusion.3
  60.7 1.1 slice.123
  61.8 2.8 %reshape.91 = f32[4,2,128,255]{3,2,0,1:T(8,128)S(1)} reshape(f32[4,2,32640]{2,0,1:T(4,128)} %slice.123) | data formatting | bytes 2088960 | tf_op jit(solution)/shard_map/while/body/eval_jaxpr/reshape | solution.py:23
  64.8 1.2 dynamic-slice_bitcast_fusion.5
  66.8 1.6 %reshape.89 = bf16[4,2,128,255]{3,2,1,0:T(8,128)(2,1)S(1)} reshape(bf16[4,2,32640]{2,1,0:T(2,128)(2,1)S(1)} %slice.122) | data formatting | bytes 1044480 | tf_op jit(solution)/shard_map/while/body/eval_jaxpr/reshape | solution.py:14
  68.4 3.4 %fusion.22 = f32[8,128,2,128]{1,3,0,2:T(8,128)} fusion(f32[8,128,2,128]{1,3,0,2:T(8,128)} %get-tuple-element.301, pred[]{:T(512)S(6)} %compare.11, bf16[8,1,128,2,128]{2,4,1,0,3:T(8,128)(2,1)S(1)} %get-tuple-element.269, bf16[8,1,128,2,128]{2,4,1,0,3:T(8,128)(2,1)} %get-tuple-element.270, bf16[8,1,128,2,128]{2,4,1,0,3:T(8,128)(2,1)} %get-tuple-element.271, ...), kind=kOutput, calls=%fused_computation.2.clone.1 | convolution fusion | flops 272105472 | bytes 4456449 | tf_op jit(solution)/shard_map/while/body/eval_jaxpr/kfts,iktfg->isfg/dot_general | solution.py:66
  71.9 1.1 convolution_bitcast_fusion.3
  75.4 2.8 %reshape.91 = f32[4,2,128,255]{3,2,0,1:T(8,128)S(1)} reshape(f32[4,2,32640]{2,0,1:T(4,128)} %slice.123) | data formatting | bytes 2088960 | tf_op jit(solution)/shard_map/while/body/eval_jaxpr/reshape | solution.py:23
  78.4 1.4 copy_multiply_fusion
  80.8 5.1 %all-to-all-start.2 = ((bf16[8,128,256]{1,2,0:T(8,128)(2,1)}), bf16[8,128,256]{1,2,0:T(8,128)(2,1)S(1)}, u32[]{:S(2)}, u32[]{:S(2)}) async-start(bf16[8,128,256]{1,2,0:T(8,128)(2,1)} %fusion.9), calls=%async_computation.2 | async-start | bytes 1048576 | tf_op jit(solution)/shard_map/all_to_all | solution.py:137
  87.0 11.8 %all-to-all-done.2 = bf16[8,128,256]{1,2,0:T(8,128)(2,1)S(1)} async-done(((bf16[8,128,256]{1,2,0:T(8,128)(2,1)}), bf16[8,128,256]{1,2,0:T(8,128)(2,1)S(1)}, u32[]{:S(2)}, u32[]{:S(2)}) %all-to-all-start.2) | async-done | bytes 524320 | tf_op jit(solution)/shard_map/all_to_all | solution.py:137
  99.8 45.9 %reduce-scatter.2.cloned.1.call-done = f32[128,16]{0,1:T(8,128)} async-done(((f32[1024,16]{0,1:T(8,128)}), f32[128,16]{0,1:T(8,128)}) %reduce-scatter.2.cloned.1.call-update) | async-done | bytes 8208 | tf_op jit(solution)/shard_map/reduce_scatter | solution.py:142
  (71 shorter events, 14.5 us)
Async XLA Ops:
  8.5 8.3 %copy-start.4 = (bf16[128,2048]{1,0:T(8,128)(2,1)S(1)}, bf16[128,2048]{1,0:T(8,128)(2,1)}, u32[]{:S(2)}) copy-start(bf16[128,2048]{1,0:T(8,128)(2,1)} %param.7) | copy-start | bytes 1572868
  9.5 21.8 %all-to-all-start = ((bf16[128,8,256]{0,2,1:T(8,128)(2,1)}), bf16[128,8,256]{0,2,1:T(8,128)(2,1)S(1)}, u32[]{:S(2)}, u32[]{:S(2)}) async-start(bf16[128,8,256]{0,2,1:T(8,128)(2,1)} %bitcast), calls=%async_computation | async-start | bytes 1048576 | tf_op jit(solution)/shard_map/all_to_all | solution.py:102
  16.8 18.1 %copy-start.7 = (bf16[128,16]{0,1:T(8,128)(2,1)S(1)}, bf16[128,16]{0,1:T(8,128)(2,1)}, u32[]{:S(2)}) copy-start(bf16[128,16]{0,1:T(8,128)(2,1)} %param.10) | copy-start | bytes 12292
  31.3 19.0 %copy-start.2 = (bf16[128,8,256]{0,2,1:T(8,128)(2,1)}, bf16[128,8,256]{0,2,1:T(8,128)(2,1)S(1)}, u32[]{:S(2)}) copy-start(bf16[128,8,256]{0,2,1:T(8,128)(2,1)S(1)} %all-to-all-done) | copy-start | bytes 1572868
  31.3 19.2 %all-to-all-start.1 = ((bf16[128,8,256]{0,2,1:T(8,128)(2,1)}), bf16[128,8,256]{0,2,1:T(8,128)(2,1)S(1)}, u32[]{:S(2)}, u32[]{:S(2)}) async-start(bf16[128,8,256]{0,2,1:T(8,128)(2,1)} %bitcast.4), calls=%async_computation.1 | async-start | bytes 1048576 | tf_op jit(solution)/shard_map/all_to_all | solution.py:103
  34.9 5.9 %collective-permute-start = (bf16[128,16]{0,1:T(8,128)(2,1)S(1)}, bf16[128,16]{0,1:T(8,128)(2,1)S(1)}, u32[]{:S(2)}, u32[]{:S(2)}) collective-permute-start(bf16[128,16]{0,1:T(8,128)(2,1)S(1)} %copy-done.7), channel_id=1, source_target_pairs={{0,2},{2,0},{4,6},{6,4},{8,10},{10,8},{12,14},{14,12},{1,3},{3,1},... | collective-permute-start | bytes 12296 | tf_op jit(solution)/shard_map/ppermute | solution.py:108
  40.8 3.7 %collective-permute-start.1 = (bf16[256,16]{0,1:T(8,128)(2,1)S(1)}, bf16[256,16]{0,1:T(8,128)(2,1)S(1)}, u32[]{:S(2)}, u32[]{:S(2)}) collective-permute-start(bf16[256,16]{0,1:T(8,128)(2,1)S(1)} %maximum_select_fusion.1), channel_id=1, source_target_pairs={{0,4},{2,6},{4,0},{6,2},{8,12},{10,14},{12,8},{14,10},{1,5},{3,7},... | collective-permute-start | bytes 24584 | tf_op jit(solution)/shard_map/ppermute | solution.py:108
  44.5 5.7 %collective-permute-start.2 = (bf16[512,16]{0,1:T(8,128)(2,1)S(1)}, bf16[512,16]{0,1:T(8,128)(2,1)S(1)}, u32[]{:S(2)}, u32[]{:S(2)}) collective-permute-start(bf16[512,16]{0,1:T(8,128)(2,1)S(1)} %maximum_select_fusion), channel_id=1, source_target_pairs={{0,8},{2,10},{4,12},{6,14},{8,0},{10,2},{12,4},{14,6},{1,9},{3,11}... | collective-permute-start | bytes 49160 | tf_op jit(solution)/shard_map/ppermute | solution.py:108
  55.1 3.1 %copy-start = (bf16[8,1,128,2,128]{2,4,1,0,3:T(8,128)(2,1)S(1)}, bf16[8,1,128,2,128]{2,4,1,0,3:T(8,128)(2,1)}, u32[]{:S(2)}) copy-start(bf16[8,1,128,2,128]{2,4,1,0,3:T(8,128)(2,1)} %get-tuple-element.270) | copy-start | bytes 1572868 | tf_op jit(solution)/shard_map/while
  55.1 3.1 %copy-start.1 = (bf16[8,1,128,2,128]{2,4,1,0,3:T(8,128)(2,1)S(1)}, bf16[8,1,128,2,128]{2,4,1,0,3:T(8,128)(2,1)}, u32[]{:S(2)}) copy-start(bf16[8,1,128,2,128]{2,4,1,0,3:T(8,128)(2,1)} %get-tuple-element.271) | copy-start | bytes 1572868 | tf_op jit(solution)/shard_map/while
  55.1 3.1 %copy-start.5 = (bf16[8,128,2,128]{3,1,0,2:T(8,128)(2,1)S(1)}, bf16[8,128,2,128]{3,1,0,2:T(8,128)(2,1)}, u32[]{:S(2)}) copy-start(bf16[8,128,2,128]{3,1,0,2:T(8,128)(2,1)} %get-tuple-element.326) | copy-start | bytes 1572868 | tf_op jit(solution)/shard_map/while
  68.4 3.5 %copy-start = (bf16[8,1,128,2,128]{2,4,1,0,3:T(8,128)(2,1)S(1)}, bf16[8,1,128,2,128]{2,4,1,0,3:T(8,128)(2,1)}, u32[]{:S(2)}) copy-start(bf16[8,1,128,2,128]{2,4,1,0,3:T(8,128)(2,1)} %get-tuple-element.270) | copy-start | bytes 1572868 | tf_op jit(solution)/shard_map/while
  68.4 3.5 %copy-start.1 = (bf16[8,1,128,2,128]{2,4,1,0,3:T(8,128)(2,1)S(1)}, bf16[8,1,128,2,128]{2,4,1,0,3:T(8,128)(2,1)}, u32[]{:S(2)}) copy-start(bf16[8,1,128,2,128]{2,4,1,0,3:T(8,128)(2,1)} %get-tuple-element.271) | copy-start | bytes 1572868 | tf_op jit(solution)/shard_map/while
  68.4 3.5 %copy-start.5 = (bf16[8,128,2,128]{3,1,0,2:T(8,128)(2,1)S(1)}, bf16[8,128,2,128]{3,1,0,2:T(8,128)(2,1)}, u32[]{:S(2)}) copy-start(bf16[8,128,2,128]{3,1,0,2:T(8,128)(2,1)} %get-tuple-element.326) | copy-start | bytes 1572868 | tf_op jit(solution)/shard_map/while
  78.4 1.4 copy-start.3
  80.8 17.9 %all-to-all-start.2 = ((bf16[8,128,256]{1,2,0:T(8,128)(2,1)}), bf16[8,128,256]{1,2,0:T(8,128)(2,1)S(1)}, u32[]{:S(2)}, u32[]{:S(2)}) async-start(bf16[8,128,256]{1,2,0:T(8,128)(2,1)} %fusion.9), calls=%async_computation.2 | async-start | bytes 1048576 | tf_op jit(solution)/shard_map/all_to_all | solution.py:137
  86.0 59.7 %reduce-scatter.2.cloned.1.call-start = ((), (), s32[]{:S(2)}) async-start(), calls=%async_computation.4 | async-start | bytes 73728 | tf_op jit(solution)/shard_map/reduce_scatter | solution.py:142
  86.4 0.6 copy-start.6
Sparse Core Ops, SparseCore 0:
  90.5 55.1 reduce-scatter.1
